TPU v7x, 256 devices: a whole 4x4x8 slice. The times are simulated.
256 devices in a mesh: req: 32 (over y, z), tp: 8 (over x, core).
Axes of the slice: x: 4, y: 4, z: 8, core: 2. Of those that a mesh axis runs over, the one named last changes fastest.
Arguments:
- tokens: bfloat16 [32768, 1792], P(('req', 'tp')), may hold values from -6 to 6
- norm_gain: float32 [1792], replicated, may hold values from 0.25 to 1.75
- ffn_gain: float32 [1792], replicated, may hold values from 0.25 to 1.75
- mix_weight: bfloat16 [1792, 4, 1792], P('req', None, 'tp'), may hold values from -0.125 to 0.125
- out_weight: bfloat16 [1792, 1792], P('tp', 'req'), may hold values from -0.125 to 0.125
- ffn_weight: bfloat16 [1792, 2, 7168], P('req', None, 'tp'), may hold values from -0.125 to 0.125
- down_weight: bfloat16 [7168, 1792], P('tp', 'req'), may hold values from -0.0625 to 0.0625
- conv_taps: float32 [3, 1792], P(None, 'tp'), may hold values from -3 to 3
- past_cache: bfloat16 [32, 2, 64, 1792], P('req', None, None, 'tp'), may hold values from -210 to 210
- cached_len: int32 [32], P('req'), may hold values from 0 to 8192, as said below
Outputs:
- layer_out: bfloat16 [32768, 1792], P(('req', 'tp'))
- new_cache: bfloat16 [32, 2, 64, 1792], P('req', None, None, 'tp')
Inputs may be any that keep to these rules, and one draw needn't show every extreme that they name: `cached_len`: one request has exactly 8192 cached positions and another fewer than 64.
All inputs are finite; a program needn't handle non-finite values.
Results may differ from a plain program's by a relative error of at most 0.02.
Values may be sent and summed in bfloat16 or wider, within the bound.
No kernel may reach another device: no remote copies, remote signals or barrier semaphores. Data moves between devices by JAX's collectives and lax.ppermute only.
A program may use at most 64 MiB of HBM per device.

v0:
```python
import math
import jax
import jax.numpy as jnp
from jax import lax
from jax.sharding import PartitionSpec as P

HD = 112
WIN = 64


def normed(row_vals, gain):
    floats = row_vals.astype(jnp.float32)
    scaled = floats * lax.rsqrt(jnp.mean(floats * floats, axis=-1, keepdims=True) + 1e-05)
    return (scaled * gain).astype(jnp.bfloat16)


def window_attend(queries, key_rows, value_rows, length, window):
    row_count, head_count, head_size = queries.shape
    nb = row_count // window
    score_scale = 1.0 / math.sqrt(head_size)
    qb = queries.reshape(nb, window, head_count, head_size)

    def blocks(rows):
        lo = rows[:row_count].reshape(nb, window, head_count, head_size)
        hi = rows[window:].reshape(nb, window, head_count, head_size)
        return jnp.concatenate([lo, hi], axis=1)

    kb = blocks(key_rows)
    vb = blocks(value_rows)
    scores = jnp.einsum("bqhd,bkhd->bhqk", qb, kb, preferred_element_type=jnp.float32) * score_scale
    i = jnp.arange(window, dtype=jnp.int32)[:, None]
    j = jnp.arange(2 * window, dtype=jnp.int32)[None, :]
    b = jnp.arange(nb, dtype=jnp.int32)[:, None, None]
    usable = (j > i)[None] & (j <= i + window)[None] & (b * window + j >= window - length)
    scores = jnp.where(usable[:, None], scores, -1e30)
    row_max = jnp.max(scores, axis=-1, keepdims=True)
    exponent = jnp.exp(scores - row_max)
    weights = (exponent / jnp.sum(exponent, axis=-1, keepdims=True)).astype(jnp.bfloat16)
    out = jnp.einsum("bhqk,bkhd->bqhd", weights, vb, preferred_element_type=jnp.float32)
    return out.reshape(row_count, head_count, head_size)


def mix_request(projected, cache_rows, length, tap_table, window, head_size):
    row_count, feat_width = (projected.shape[0], projected.shape[2])
    time_order = (length + jnp.arange(window, dtype=jnp.int32)) % window
    earlier = cache_rows[:, time_order]
    key_rows = jnp.concatenate([earlier[0], projected[:, 1]], axis=0)
    value_rows = jnp.concatenate([earlier[1], projected[:, 2]], axis=0)
    head_count = feat_width // head_size
    attended = window_attend(
        projected[:, 0].reshape(row_count, head_count, head_size),
        key_rows.reshape(-1, head_count, head_size),
        value_rows.reshape(-1, head_count, head_size),
        length,
        window,
    ).reshape(row_count, feat_width)
    positions = jnp.arange(window + row_count, dtype=jnp.int32)
    alive_mask = (positions >= window - length)[:, None]
    masked_values = jnp.where(alive_mask, value_rows.astype(jnp.float32), jnp.float32(0.0))
    tap_count = tap_table.shape[0]
    convolved = jnp.zeros((row_count, feat_width), jnp.float32)
    for tap_index in range(tap_count):
        begin_row = window - (tap_count - 1) + tap_index
        convolved = (
            convolved + tap_table[tap_index] * masked_values[begin_row : begin_row + row_count]
        )
    mixed_heads = (attended + projected[:, 3].astype(jnp.float32) * convolved).astype(jnp.bfloat16)
    slot_source = (
        row_count - window + (jnp.arange(window, dtype=jnp.int32) - length - row_count) % window
    )
    renewed = jnp.stack([projected[:, 1], projected[:, 2]])[:, slot_source]
    return (mixed_heads, renewed)


def gather_packed(pieces):
    widths = [p.shape[1] for p in pieces]
    got = lax.all_gather(jnp.concatenate(pieces, axis=1), "req", axis=0, tiled=True)
    parts = []
    start = 0
    for w in widths:
        parts.append(got[:, start : start + w])
        start += w
    return parts


def core_swap(x):
    return lax.ppermute(x, "tpc", [(0, 1), (1, 0)])


def mlp_rows(rows, ffn_all, down_t, ffn_width):
    gate_up = jnp.dot(rows, ffn_all, preferred_element_type=jnp.float32)
    activated = (jax.nn.silu(gate_up[:, :ffn_width]) * gate_up[:, ffn_width:]).astype(jnp.bfloat16)
    out = lax.dot_general(
        activated, down_t, (((1,), (1,)), ((), ())), preferred_element_type=jnp.float32
    )
    return out.astype(jnp.bfloat16)


def local(
    tokens,
    norm_gain,
    ffn_gain,
    mix_weight,
    out_weight,
    ffn_weight,
    down_weight,
    conv_taps,
    past_cache,
    cached_len,
):
    feat_width = mix_weight.shape[2]
    ffn_width = ffn_weight.shape[2]
    rows = mix_weight.shape[0]
    mix_all, out_t = gather_packed([mix_weight.reshape(rows, -1), out_weight.T])
    ffn_all, down_t = gather_packed([ffn_weight.reshape(rows, -1), down_weight.T])
    nxt = lax.axis_size("tpx")
    tok_mine = lax.all_to_all(
        jnp.tile(normed(tokens, norm_gain)[None], (nxt, 1, 1)), "tpx", 0, 0, tiled=True
    )
    tok_theirs = core_swap(tok_mine)
    first = lax.axis_index("tpc") == 0
    pairs = jnp.stack(
        [jnp.where(first, tok_mine, tok_theirs), jnp.where(first, tok_theirs, tok_mine)], axis=1
    )
    normed_all = pairs.reshape((-1,) + tok_mine.shape[2:])
    row_total = normed_all.shape[0]
    projected = jnp.dot(normed_all, mix_all, preferred_element_type=jnp.float32)
    projected = projected.astype(jnp.bfloat16).reshape(row_total, 4, feat_width)
    mixed_heads, renewed = mix_request(projected, past_cache[0], cached_len[0], conv_taps, WIN, HD)
    nx = lax.axis_size("tpx")
    nc = lax.axis_size("tpc")
    me_c = lax.axis_index("tpc")
    by_core = mixed_heads.reshape(nx, nc, -1, feat_width)
    mine_rows = lax.dynamic_index_in_dim(by_core, me_c, axis=1, keepdims=False)
    their_rows = lax.dynamic_index_in_dim(by_core, 1 - me_c, axis=1, keepdims=False)

    def out_rows(r):
        return lax.dot_general(
            r.reshape(-1, feat_width),
            out_t,
            (((1,), (1,)), ((), ())),
            preferred_element_type=jnp.float32,
        ).astype(jnp.bfloat16)

    back = core_swap(out_rows(their_rows))
    pair = (out_rows(mine_rows).astype(jnp.float32) + back.astype(jnp.float32)).astype(jnp.bfloat16)
    chips = lax.all_to_all(pair.reshape((nx, -1) + pair.shape[1:]), "tpx", 0, 0, tiled=True)
    attn_part = chips.astype(jnp.float32).sum(axis=0)
    residual = (tokens.astype(jnp.float32) + attn_part).astype(jnp.bfloat16)
    nx = lax.axis_size("tpx")
    mine = lax.all_to_all(
        jnp.tile(normed(residual, ffn_gain)[None], (nx, 1, 1)), "tpx", 0, 0, tiled=True
    )
    flat = mine.reshape((-1,) + mine.shape[2:])
    theirs = core_swap(flat)
    part_mine = mlp_rows(flat, ffn_all, down_t, ffn_width)
    part_theirs = mlp_rows(theirs, ffn_all, down_t, ffn_width)
    back = core_swap(part_theirs)
    pair = (part_mine.astype(jnp.float32) + back.astype(jnp.float32)).astype(jnp.bfloat16)
    cols = pair.shape[1] // 2
    on_sc = lax.psum_scatter(pair[:, :cols], "tpx", scatter_dimension=0, tiled=True)
    by_a2a = lax.all_to_all(pair[:, cols:].reshape((nx, -1, cols)), "tpx", 0, 0, tiled=True)
    ffn_part = jnp.concatenate(
        [on_sc.astype(jnp.float32), by_a2a.astype(jnp.float32).sum(axis=0)], axis=1
    )
    layer_out = (residual.astype(jnp.float32) + ffn_part).astype(jnp.bfloat16)
    return (layer_out, renewed[None])


def solution(mesh):
    n_req, n_tp = mesh.devices.shape
    split = jax.sharding.Mesh(mesh.devices.reshape(n_req, n_tp // 2, 2), ("req", "tpx", "tpc"))
    tp = ("tpx", "tpc")
    in_specs = (
        P(("req",) + tp, None),
        P(),
        P(),
        P("req", None, tp),
        P(tp, "req"),
        P("req", None, tp),
        P(tp, "req"),
        P(None, tp),
        P("req", None, None, tp),
        P("req"),
    )
    out_specs = (P(("req",) + tp, None), P("req", None, None, tp))
    return jax.shard_map(local, mesh=split, in_specs=in_specs, out_specs=out_specs, check_vma=False)
```

profile of v0, /device:TPU:1, one launch (start us, length us, event | category | flops | bytes accessed | tf_op | source)
XLA Modules:
  0.0 253.3 jit_solution(17294180878208792725)
XLA Ops:
  8.3 1.4 pad_maximum_fusion.5
  10.8 1.6 pad_maximum_fusion.4
  13.0 27.3 %all_to_all.20 = bf16[4,128,1792]{2,1,0:T(8,128)(2,1)S(1)} all-to-all(bf16[4,128,1792]{2,1,0:T(8,128)(2,1)S(1)} %tile.4), channel_id=1, replica_groups=mesh['req'=32,'tpx'=4,'tpc'=2] {'tpx'}, dimensions={0} | all-to-all | bytes 3670016 | tf_op jit(solution)/shard_map/all_to_all | solution.py:117
  40.3 2.0 collective-permute-start
  45.8 1.7 select_bitcast_fusion.1
  47.6 2.1 pad_maximum_fusion
  49.6 44.5 %all-gather.3.cloned.1.call-done = bf16[1792,1120]{1,0:T(8,128)(2,1)} async-done(((bf16[56,1120]{1,0:T(8,128)(2,1)}), bf16[1792,1120]{1,0:T(8,128)(2,1)}) %all-gather.3.cloned.1.call-update) | async-done | bytes 4014096 | tf_op jit(solution)/shard_map/all_gather | solution.py:77
  94.1 6.6 %fusion.13 = bf16[1024,896]{0,1:T(8,128)(2,1)S(1)} fusion(bf16[1024,1792]{1,0:T(8,128)(2,1)} %bitcast.68, bf16[1792,1120]{1,0:T(8,128)(2,1)} %all-gather.3.cloned.1.call-done), kind=kOutput, calls=%fused_computation.26 | convolution fusion | flops 3289251840 | bytes 8716288 | tf_op jit(solution)/shard_map/dot_general | solution.py:127
  103.9 2.6 %reshape.295 = bf16[16,64,2,112]{1,0,3,2:T(8,128)(2,1)} reshape(bf16[1024,1,224]{0,2,1:T(8,128)(2,1)} %get-tuple-element.14) | data formatting | bytes 917504 | tf_op jit(solution)/shard_map/reshape;reshape;squeeze | solution.py:21
  109.7 2.2 reshape.267
  111.9 2.1 copy.32
  114.1 2.1 copy.33
  116.2 2.4 fusion.69
  118.7 3.0 %fusion.18 = f32[16,2,64,128]{3,2,1,0:T(8,128)} fusion(bf16[16,64,2,112]{1,3,2,0:T(8,128)(2,1)S(1)} %copy.39, bf16[16,64,2,112]{1,3,2,0:T(8,128)(2,1)S(1)} %copy.38, bf16[16,64,2,112]{1,0,3,2:T(8,128)(2,1)} %reshape.295, pred[16,64,128]{2,1,0:T(8,128)(4,1)S(1)} %broadcast_and_fusion), kind=kOutput, calls=%fused_computation.36 | convolution fusion | flops 61079552 | bytes 2555904 | tf_op jit(solution)/shard_map/bqhd,bkhd->bhqk/dot_general | solution.py:30
  121.7 6.3 %convolution_bitcast_fusion = f32[16,64,2,112]{3,1,2,0:T(8,128)S(1)} fusion(bf16[16,64,2,112]{1,3,2,0:T(8,128)(2,1)} %copy.33, bf16[16,64,2,112]{1,3,2,0:T(8,128)(2,1)} %copy.32, f32[16,2,64]{2,1,0:T(2,128)S(1)} %fusion.69, f32[16,2,64,128]{3,2,1,0:T(8,128)} %fusion.18), kind=kOutput, calls=%fused_computation.37 | convolution fusion | flops 61343872 | bytes 2891776 | tf_op jit(solution)/shard_map/bhqk,bkhd->bqhd/dot_general | solution.py:39
  131.1 1.9 convolution_convert_fusion
  133.0 3.3 %collective-permute-start.1 = (bf16[512,1792]{1,0:T(8,128)(2,1)S(1)}, bf16[512,1792]{1,0:T(8,128)(2,1)S(1)}, u32[]{:S(2)}, u32[]{:S(2)}) collective-permute-start(bf16[512,1792]{1,0:T(8,128)(2,1)S(1)} %convolution_convert_fusion), channel_id=1, source_target_pairs={{0,1},{1,0},{2,3},{3,2},{4,5},{5,4},{6,7},{7,6},{8,9},{9,8},{10,11... | collective-permute-start | bytes 5505032 | tf_op jit(solution)/shard_map/ppermute | solution.py:87
  136.3 3.4 %collective-permute-done.1 = bf16[512,1792]{1,0:T(8,128)(2,1)S(1)} collective-permute-done((bf16[512,1792]{1,0:T(8,128)(2,1)S(1)}, bf16[512,1792]{1,0:T(8,128)(2,1)S(1)}, u32[]{:S(2)}, u32[]{:S(2)}) %collective-permute-start.1) | collective-permute-done | bytes 1835040 | tf_op jit(solution)/shard_map/ppermute | solution.py:87
  139.7 1.9 add_convert_fusion.1
  141.6 26.5 %all_to_all.21 = bf16[4,128,1792]{2,1,0:T(8,128)(2,1)S(1)} all-to-all(bf16[4,128,1792]{2,1,0:T(8,128)(2,1)S(1)} %bitcast.67), channel_id=1, replica_groups=mesh['req'=32,'tpx'=4,'tpc'=2] {'tpx'}, dimensions={0} | all-to-all | bytes 3670016 | tf_op jit(solution)/shard_map/all_to_all | solution.py:147
  169.1 24.2 %all_to_all.22 = bf16[4,128,1792]{2,1,0:T(8,128)(2,1)S(1)} all-to-all(bf16[4,128,1792]{2,1,0:T(8,128)(2,1)S(1)} %tile.5), channel_id=1, replica_groups=mesh['req'=32,'tpx'=4,'tpc'=2] {'tpx'}, dimensions={0} | all-to-all | bytes 3670016 | tf_op jit(solution)/shard_map/all_to_all | solution.py:151
  193.3 2.7 %collective-permute-start.2 = (bf16[512,1792]{1,0:T(8,128)(2,1)S(1)}, bf16[512,1792]{1,0:T(8,128)(2,1)}, u32[]{:S(2)}, u32[]{:S(2)}) collective-permute-start(bf16[512,1792]{1,0:T(8,128)(2,1)S(1)} %bitcast.70), channel_id=1, source_target_pairs={{0,1},{1,0},{2,3},{3,2},{4,5},{5,4},{6,7},{7,6},{8,9},{9,8},{10,11... | collective-permute-start | bytes 5505032 | tf_op jit(solution)/shard_map/ppermute | solution.py:87
  196.0 3.5 %collective-permute-done.2 = bf16[512,1792]{1,0:T(8,128)(2,1)} collective-permute-done((bf16[512,1792]{1,0:T(8,128)(2,1)S(1)}, bf16[512,1792]{1,0:T(8,128)(2,1)}, u32[]{:S(2)}, u32[]{:S(2)}) %collective-permute-start.2) | collective-permute-done | bytes 1835040 | tf_op jit(solution)/shard_map/ppermute | solution.py:87
  200.7 7.0 %fusion.1 = f32[512,1792]{1,0:T(8,128)S(1)} fusion(bf16[512,1792]{1,0:T(8,128)(2,1)} %collective-permute-done.2, bf16[1792,2688]{1,0:T(8,128)(2,1)} %all-gather.5.cloned.1.call-done), kind=kOutput, calls=%fused_computation.3 | convolution fusion | flops 3288334336 | bytes 11927552 | tf_op jit(solution)/shard_map/dot_general | solution.py:91
  207.8 2.3 convolution_convert_fusion.2
  211.3 3.5 %fusion.3 = f32[512,1792]{1,0:T(8,128)S(1)} fusion(bf16[512,1792]{1,0:T(8,128)(2,1)S(1)} %bitcast.71, bf16[1792,2688]{1,0:T(8,128)(2,1)S(1)} %copy-done.9), kind=kOutput, calls=%fused_computation.5 | convolution fusion | flops 3288334336 | bytes 11927552 | tf_op jit(solution)/shard_map/dot_general | solution.py:91
  214.8 2.3 add_convert_fusion
  217.1 1.4 fusion.66
  218.6 4.6 %all-to-all-start.3 = ((bf16[4,128,896]{2,1,0:T(8,128)(2,1)}), bf16[4,128,896]{2,1,0:T(8,128)(2,1)}, u32[]{:S(2)}, u32[]{:S(2)}) async-start(bf16[4,128,896]{2,1,0:T(8,128)(2,1)} %bitcast.22), calls=%async_computation.4 | async-start | bytes 1835008 | tf_op jit(solution)/shard_map/all_to_all | solution.py:162
  224.9 3.4 %pad_maximum_fusion.1 = bf16[2,1024,224]{2,0,1:T(2,128)(2,1)} fusion(bf16[1,1024,224]{2,0,1:T(2,128)(2,1)S(1)} %copy.47, bf16[1,1024,224]{2,0,1:T(2,128)(2,1)S(1)} %copy.46), kind=kLoop, calls=%fused_computation.47 | loop fusion | flops 1835008 | bytes 1835008 | tf_op jit(solution)/shard_map/stack | solution.py:71
  228.3 1.9 gather_fusion.1
  230.9 11.7 %all-to-all-done.3 = bf16[4,128,896]{2,1,0:T(8,128)(2,1)} async-done(((bf16[4,128,896]{2,1,0:T(8,128)(2,1)}), bf16[4,128,896]{2,1,0:T(8,128)(2,1)}, u32[]{:S(2)}, u32[]{:S(2)}) %all-to-all-start.3) | async-done | bytes 917536 | tf_op jit(solution)/shard_map/all_to_all | solution.py:162
  (78 shorter events, 24.9 us)
Async XLA Ops:
  7.2 5.3 %copy-start = (bf16[128,1792]{1,0:T(8,128)(2,1)S(1)}, bf16[128,1792]{1,0:T(8,128)(2,1)}, u32[]{:S(2)}) copy-start(bf16[128,1792]{1,0:T(8,128)(2,1)} %param.10) | copy-start | bytes 1376260
  7.2 5.5 %copy-start.5 = (f32[1792]{0:T(1024)S(1)}, f32[1792]{0:T(1024)}, u32[]{:S(2)}) copy-start(f32[1792]{0:T(1024)} %param.11) | copy-start | bytes 21508
  7.2 86.9 %all-gather.3.cloned.1.call-start = ((), (), s32[]{:S(2)}) async-start(), calls=%async_computation.5 | async-start | bytes 4257792 | tf_op jit(solution)/shard_map/all_gather | solution.py:77
  9.8 191.0 %all-gather.5.cloned.1.call-start = ((), (), s32[]{:S(2)}) async-start(), calls=%async_computation.6 | async-start | bytes 9934848 | tf_op jit(solution)/shard_map/all_gather | solution.py:77
  12.4 232.5 %reduce-scatter.2.cloned.1.call-start = ((), (), s32[]{:S(2)}) async-start(), calls=%async_computation.7 | async-start | bytes 1146880 | tf_op jit(solution)/shard_map/reduce_scatter | solution.py:161
  13.0 29.9 %copy-start.4 = (bf16[1,2,64,224]{3,2,1,0:T(8,128)(2,1)S(1)}, bf16[1,2,64,224]{3,2,1,0:T(8,128)(2,1)}, u32[]{:S(2)}) copy-start(bf16[1,2,64,224]{3,2,1,0:T(8,128)(2,1)} %param.18) | copy-start | bytes 172036
  13.0 31.7 %copy-start.7 = (f32[3,224]{1,0:T(4,128)S(1)}, f32[3,224]{1,0:T(4,128)}, u32[]{:S(2)}) copy-start(f32[3,224]{1,0:T(4,128)} %param.17) | copy-start | bytes 8068
  40.3 5.5 %collective-permute-start = (bf16[4,128,1792]{2,1,0:T(8,128)(2,1)S(1)}, bf16[4,128,1792]{2,1,0:T(8,128)(2,1)}, u32[]{:S(2)}, u32[]{:S(2)}) collective-permute-start(bf16[4,128,1792]{2,1,0:T(8,128)(2,1)S(1)} %all_to_all.20), channel_id=1, source_target_pairs={{0,1},{1,0},{2,3},{3,2},{4,5},{5,4},{6,7},{7,6},{8,9},{9,8},{10,11... | collective-permute-start | bytes 5505032 | tf_op jit(solution)/shard_map/ppermute | solution.py:87
  44.5 64.3 %copy-start.3 = (bf16[1,64,224]{2,1,0:T(8,128)(2,1)}, bf16[1,64,224]{2,1,0:T(8,128)(2,1)S(1)}, u32[]{:S(2)}) copy-start(bf16[1,64,224]{2,1,0:T(8,128)(2,1)S(1)} %copy.75) | copy-start | bytes 86020
  128.0 1.4 copy-start.2
  133.0 6.7 %collective-permute-start.1 = (bf16[512,1792]{1,0:T(8,128)(2,1)S(1)}, bf16[512,1792]{1,0:T(8,128)(2,1)S(1)}, u32[]{:S(2)}, u32[]{:S(2)}) collective-permute-start(bf16[512,1792]{1,0:T(8,128)(2,1)S(1)} %convolution_convert_fusion), channel_id=1, source_target_pairs={{0,1},{1,0},{2,3},{3,2},{4,5},{5,4},{6,7},{7,6},{8,9},{9,8},{10,11... | collective-permute-start | bytes 5505032 | tf_op jit(solution)/shard_map/ppermute | solution.py:87
  168.1 0.7 copy-start.6
  193.3 6.2 %collective-permute-start.2 = (bf16[512,1792]{1,0:T(8,128)(2,1)S(1)}, bf16[512,1792]{1,0:T(8,128)(2,1)}, u32[]{:S(2)}, u32[]{:S(2)}) collective-permute-start(bf16[512,1792]{1,0:T(8,128)(2,1)S(1)} %bitcast.70), channel_id=1, source_target_pairs={{0,1},{1,0},{2,3},{3,2},{4,5},{5,4},{6,7},{7,6},{8,9},{9,8},{10,11... | collective-permute-start | bytes 5505032 | tf_op jit(solution)/shard_map/ppermute | solution.py:87
  200.7 7.0 %copy-start.9 = (bf16[1792,2688]{1,0:T(8,128)(2,1)S(1)}, bf16[1792,2688]{1,0:T(8,128)(2,1)}, u32[]{:S(2)}) copy-start(bf16[1792,2688]{1,0:T(8,128)(2,1)} %all-gather.5.cloned.1.call-done) | copy-start | bytes 28901380
  210.1 4.7 %collective-permute-start.3 = (bf16[512,1792]{1,0:T(8,128)(2,1)S(1)}, bf16[512,1792]{1,0:T(8,128)(2,1)S(1)}, u32[]{:S(2)}, u32[]{:S(2)}) collective-permute-start(bf16[512,1792]{1,0:T(8,128)(2,1)S(1)} %convolution_convert_fusion.2), channel_id=1, source_target_pairs={{0,1},{1,0},{2,3},{3,2},{4,5},{5,4},{6,7},{7,6},{8,9},{9,8},{10,11... | collective-permute-start | bytes 5505032 | tf_op jit(solution)/shard_map/ppermute | solution.py:87
  218.5 4.7 %copy-start.8 = (s32[64]{0:T(128)S(1)}, s32[64]{0:T(128)}, u32[]{:S(2)}) copy-start(s32[64]{0:T(128)} %get-tuple-element.26) | copy-start | bytes 772
  218.6 5.5 %copy-start.1 = (bf16[1,1024,224]{1,2,0:T(8,128)(2,1)S(1)}, bf16[1,1024,224]{1,2,0:T(8,128)(2,1)}, u32[]{:S(2)}) copy-start(bf16[1,1024,224]{1,2,0:T(8,128)(2,1)} %get-tuple-element.10) | copy-start | bytes 1376260
  218.6 24.0 %all-to-all-start.3 = ((bf16[4,128,896]{2,1,0:T(8,128)(2,1)}), bf16[4,128,896]{2,1,0:T(8,128)(2,1)}, u32[]{:S(2)}, u32[]{:S(2)}) async-start(bf16[4,128,896]{2,1,0:T(8,128)(2,1)} %bitcast.22), calls=%async_computation.4 | async-start | bytes 1835008 | tf_op jit(solution)/shard_map/all_to_all | solution.py:162
Sparse Core Ops, SparseCore 0:
  11.2 82.8 all-gather.2
  96.7 103.9 all-gather.4
  218.7 26.1 reduce-scatter.1
where the time goes:
time: 254 us; the launch traced here: 253 us
  blocking collectives  78 us (31%)
  waiting for transfers between devices  66.3 us (26%)
  matrix products  37.2 us (15%)
  local copies, waits for them, and re-layouts  25.3 us (10%)
  other arithmetic  17.8 us (7%)
  between operations  14.8 us (6%)
  starting transfers between devices  13.9 us (5%)
    all_gather x2, waiting for transfers between devices, gather_packed(): lax.all_gather(jnp.concatenate(pieces, axis=1), 'req', axis=0, tiled=True)  45.7 us
    all_to_all x1, blocking collectives, local(): lax.all_to_all(jnp.tile(normed(tokens, norm_gain)[None], (nxt, 1, 1)), 't...  27.3 us
    all_to_all x1, blocking collectives, local(): lax.all_to_all(pair.reshape((nx, -1) + pair.shape[1:]), 'tpx', 0, 0, tile...  26.5 us
    all_to_all x1, blocking collectives, local(): lax.all_to_all(jnp.tile(normed(residual, ffn_gain)[None], (nx, 1, 1)), 't...  24.2 us
    all_to_all x1, waiting for transfers between devices, local(): lax.all_to_all(pair[:, cols:].reshape((nx, -1, cols)), 'tpx', 0, 0, tiled...  11.7 us
    dot_general x2, matrix products, mlp_rows(): gate_up = jnp.dot(rows, ffn_all, preferred_element_type=jnp.float32)  10.5 us
    ppermute x4, starting transfers between devices, core_swap(): return lax.ppermute(x, 'tpc', [(0, 1), (1, 0)])  9.13 us
    ppermute x4, waiting for transfers between devices, core_swap(): return lax.ppermute(x, 'tpc', [(0, 1), (1, 0)])  7.95 us
  transfers between devices with their start and end apart: 8, of which 7 were waited for; matrix products, arithmetic and copies ran while one was open for 25% of the time, Pallas kernels for 0%

commit v1 on v0

--- a/solution.py
+++ b/solution.py
@@ -74,7 +74,12 @@
 
 def gather_packed(pieces):
     widths = [p.shape[1] for p in pieces]
-    got = lax.all_gather(jnp.concatenate(pieces, axis=1), "req", axis=0, tiled=True)
+    got = jnp.concatenate(
+        lax.all_to_all(
+            jnp.stack([jnp.concatenate(pieces, axis=1)] * lax.axis_size("req")), "req", 0, 0
+        ),
+        axis=0,
+    )
     parts = []
     start = 0
     for w in widths:

time: 254 us -> 527 us (2.07)
  waiting for transfers between devices: 66.3 us -> 362 us
  blocking collectives: 78 us -> 25.7 us
  starting transfers between devices: 13.9 us -> 38.6 us
    all_to_all x0 -> x4, waiting for transfers between devices: none -> 340 us  [the longest x2 297 us: gather_packed(): lax.all_to_all(jnp.stack([jnp.concatenate(pieces, axis=1)] * lax.axis_siz...]
    all_to_all x2 -> x0, blocking collectives: 51.5 us -> none  [the longest x1 27.3 us: local(): lax.all_to_all(jnp.tile(normed(tokens, norm_gain)[None], (nxt, 1, 1)), 't...]
    all_gather x2 -> x0, waiting for transfers between devices: 45.7 us -> none  [gather_packed(): lax.all_gather(jnp.concatenate(pieces, axis=1), 'req', axis=0, tiled=True)]
    all_to_all x0 -> x4, starting transfers between devices: none -> 26.1 us  [the longest x2 17.4 us: gather_packed(): lax.all_to_all(jnp.stack([jnp.concatenate(pieces, axis=1)] * lax.axis_siz...]
    another operation x0 -> x2, local copies, waits for them, and re-layouts: none -> 6.57 us  [gather_packed(): jnp.stack([jnp.concatenate(pieces, axis=1)] * lax.axis_size('req'))]
  transfers between devices with their start and end apart: 8 -> 10, of which waited for: 7 -> 9; matrix products, arithmetic and copies ran while one was open for 25% -> 4% of each run, Pallas kernels for 0% -> 0%
where the time goes in v1:
time: 527 us; the launch traced here: 523 us
  waiting for transfers between devices  362 us (69%)
  matrix products  40.8 us (8%)
  starting transfers between devices  38.6 us (7%)
  local copies, waits for them, and re-layouts  26.3 us (5%)
  blocking collectives  25.7 us (5%)
  between operations  15.1 us (3%)
  other arithmetic  14.8 us (3%)
    all_to_all x2, waiting for transfers between devices, gather_packed(): lax.all_to_all(jnp.stack([jnp.concatenate(pieces, axis=1)] * lax.axis_siz...  297 us
    all_to_all x1, blocking collectives, local(): lax.all_to_all(pair.reshape((nx, -1) + pair.shape[1:]), 'tpx', 0, 0, tile...  25.7 us
    all_to_all x1, waiting for transfers between devices, local(): lax.all_to_all(jnp.tile(normed(residual, ffn_gain)[None], (nx, 1, 1)), 't...  22.2 us
    all_to_all x1, waiting for transfers between devices, local(): lax.all_to_all(jnp.tile(normed(tokens, norm_gain)[None], (nxt, 1, 1)), 't...  21.4 us
    all_to_all x2, starting transfers between devices, gather_packed(): lax.all_to_all(jnp.stack([jnp.concatenate(pieces, axis=1)] * lax.axis_siz...  17.4 us
    dot_general x2, matrix products, mlp_rows(): gate_up = jnp.dot(rows, ffn_all, preferred_element_type=jnp.float32)  13.2 us
    all_to_all x1, waiting for transfers between devices, local(): lax.all_to_all(pair[:, cols:].reshape((nx, -1, cols)), 'tpx', 0, 0, tiled...  11.1 us
  transfers between devices with their start and end apart: 10, of which 9 were waited for; matrix products, arithmetic and copies ran while one was open for 4% of the time, Pallas kernels for 0%

profile of v1, /device:TPU:1, one launch (start us, length us, event | category | flops | bytes accessed | tf_op | source)
XLA Modules:
  0.0 523.0 jit_solution(14560421678901557401)
XLA Ops:
  11.0 5.0 all-to-all-start
  16.1 21.4 %all-to-all-done = bf16[4,128,1792]{2,1,0:T(8,128)(2,1)S(1)} async-done(((bf16[4,128,1792]{2,1,0:T(8,128)(2,1)}), bf16[4,128,1792]{2,1,0:T(8,128)(2,1)S(1)}, u32[]{:S(2)}, u32[]{:S(2)}) %all-to-all-start) | async-done | bytes 1835040 | tf_op jit(solution)/shard_map/all_to_all | solution.py:122
  37.5 2.2 stack.15
  39.8 12.5 %all-to-all-start.1 = ((bf16[32,56,1120]{2,1,0:T(8,128)(2,1)}), bf16[32,56,1120]{2,1,0:T(8,128)(2,1)}, u32[]{:S(2)}, u32[]{:S(2)}) async-start(bf16[32,56,1120]{2,1,0:T(8,128)(2,1)} %stack.15), calls=%async_computation.1 | async-start | bytes 8257536 | tf_op jit(solution)/shard_map/all_to_all | solution.py:78
  52.3 2.2 collective-permute-start
  58.0 1.7 select_bitcast_fusion.1
  59.8 2.2 pad_maximum_fusion
  61.9 85.5 %all-to-all-done.1 = bf16[32,56,1120]{2,1,0:T(8,128)(2,1)} async-done(((bf16[32,56,1120]{2,1,0:T(8,128)(2,1)}), bf16[32,56,1120]{2,1,0:T(8,128)(2,1)}, u32[]{:S(2)}, u32[]{:S(2)}) %all-to-all-start.1) | async-done | bytes 4014112 | tf_op jit(solution)/shard_map/all_to_all | solution.py:78
  147.4 6.6 %fusion.13 = bf16[1024,896]{0,1:T(8,128)(2,1)S(1)} fusion(bf16[1024,1792]{1,0:T(8,128)(2,1)} %bitcast.70, bf16[1792,1120]{1,0:T(8,128)(2,1)} %bitcast.9), kind=kOutput, calls=%fused_computation.26 | convolution fusion | flops 3289251840 | bytes 8716288 | tf_op jit(solution)/shard_map/dot_general | solution.py:132
  157.1 1.9 reshape.307
  160.3 1.8 fusion.18
  164.1 5.7 %convolution_bitcast_fusion = f32[16,64,2,112]{3,1,2,0:T(8,128)S(1)} fusion(bf16[16,64,2,112]{1,3,2,0:T(8,128)(2,1)S(1)} %copy.33, bf16[16,64,2,112]{1,3,2,0:T(8,128)(2,1)S(1)} %copy.32, f32[16,2,64]{2,1,0:T(2,128)S(1)} %fusion.69, f32[16,2,64,128]{3,2,1,0:T(8,128)} %fusion.18), kind=kOutput, calls=%fused_computation.37 | convolution fusion | flops 61343872 | bytes 2891776 | tf_op jit(solution)/shard_map/bhqk,bkhd->bqhd/dot_general | solution.py:39
  173.2 1.9 convolution_convert_fusion
  175.1 1.6 collective-permute-start.1
  176.7 3.4 collective-permute-done.1
  180.2 1.9 add_convert_fusion.1
  182.0 25.7 %all_to_all.30 = bf16[4,128,1792]{2,1,0:T(8,128)(2,1)S(1)} all-to-all(bf16[4,128,1792]{2,1,0:T(8,128)(2,1)S(1)} %bitcast.69), channel_id=1, replica_groups=mesh['req'=32,'tpx'=4,'tpc'=2] {'tpx'}, dimensions={0} | all-to-all | bytes 3670016 | tf_op jit(solution)/shard_map/all_to_all | solution.py:152
  210.6 3.7 all-to-all-start.3
  214.4 22.2 %all-to-all-done.3 = bf16[4,128,1792]{2,1,0:T(8,128)(2,1)S(1)} async-done(((bf16[4,128,1792]{2,1,0:T(8,128)(2,1)}), bf16[4,128,1792]{2,1,0:T(8,128)(2,1)S(1)}, u32[]{:S(2)}, u32[]{:S(2)}) %all-to-all-start.3) | async-done | bytes 1835040 | tf_op jit(solution)/shard_map/all_to_all | solution.py:156
  236.6 4.3 stack.16
  241.0 5.0 all-to-all-start.4
  246.0 2.4 collective-permute-start.2
  248.4 3.5 collective-permute-done.2
  252.0 211.3 %all-to-all-done.4 = bf16[32,56,2688]{2,1,0:T(8,128)(2,1)} async-done(((bf16[32,56,2688]{2,1,0:T(8,128)(2,1)}), bf16[32,56,2688]{2,1,0:T(8,128)(2,1)}, u32[]{:S(2)}, u32[]{:S(2)}) %all-to-all-start.4) | async-done | bytes 9633824 | tf_op jit(solution)/shard_map/all_to_all | solution.py:78
  463.2 6.9 %fusion.1 = f32[512,1792]{1,0:T(8,128)S(1)} fusion(bf16[512,1792]{1,0:T(8,128)(2,1)} %collective-permute-done.2, bf16[1792,2688]{1,0:T(8,128)(2,1)} %bitcast.23), kind=kOutput, calls=%fused_computation.3 | convolution fusion | flops 3288334336 | bytes 11927552 | tf_op jit(solution)/shard_map/dot_general | solution.py:96
  470.1 4.2 convolution_convert_fusion.2
  475.9 6.3 %fusion.3 = f32[512,1792]{1,0:T(8,128)S(1)} fusion(bf16[512,1792]{1,0:T(8,128)(2,1)S(1)} %bitcast.73, bf16[1792,2688]{1,0:T(8,128)(2,1)} %bitcast.23), kind=kOutput, calls=%fused_computation.5 | convolution fusion | flops 3288334336 | bytes 11927552 | tf_op jit(solution)/shard_map/dot_general | solution.py:96
  482.2 4.3 add_convert_fusion
  487.9 4.6 all-to-all-start.5
  494.3 3.4 pad_maximum_fusion.1
  497.7 1.9 gather_fusion.1
  500.3 11.1 %all-to-all-done.5 = bf16[4,128,896]{2,1,0:T(8,128)(2,1)} async-done(((bf16[4,128,896]{2,1,0:T(8,128)(2,1)}), bf16[4,128,896]{2,1,0:T(8,128)(2,1)}, u32[]{:S(2)}, u32[]{:S(2)}) %all-to-all-start.5) | async-done | bytes 917536 | tf_op jit(solution)/shard_map/all_to_all | solution.py:167
  (78 shorter events, 29.4 us)
Async XLA Ops:
  11.0 5.0 copy-start.3
  11.0 5.1 copy-start.6
  11.0 26.6 %all-to-all-start = ((bf16[4,128,1792]{2,1,0:T(8,128)(2,1)}), bf16[4,128,1792]{2,1,0:T(8,128)(2,1)S(1)}, u32[]{:S(2)}, u32[]{:S(2)}) async-start(bf16[4,128,1792]{2,1,0:T(8,128)(2,1)} %tile.4), calls=%async_computation | async-start | bytes 3670016 | tf_op jit(solution)/shard_map/all_to_all | solution.py:122
  39.8 14.7 %copy-start.5 = (bf16[1,2,64,224]{3,2,1,0:T(8,128)(2,1)S(1)}, bf16[1,2,64,224]{3,2,1,0:T(8,128)(2,1)}, u32[]{:S(2)}) copy-start(bf16[1,2,64,224]{3,2,1,0:T(8,128)(2,1)} %param.18) | copy-start | bytes 172036
  39.8 16.5 %copy-start.8 = (f32[3,224]{1,0:T(4,128)S(1)}, f32[3,224]{1,0:T(4,128)}, u32[]{:S(2)}) copy-start(f32[3,224]{1,0:T(4,128)} %param.17) | copy-start | bytes 8068
  39.8 107.6 %all-to-all-start.1 = ((bf16[32,56,1120]{2,1,0:T(8,128)(2,1)}), bf16[32,56,1120]{2,1,0:T(8,128)(2,1)}, u32[]{:S(2)}, u32[]{:S(2)}) async-start(bf16[32,56,1120]{2,1,0:T(8,128)(2,1)} %stack.15), calls=%async_computation.1 | async-start | bytes 8257536 | tf_op jit(solution)/shard_map/all_to_all | solution.py:78
  52.3 5.8 %collective-permute-start = (bf16[4,128,1792]{2,1,0:T(8,128)(2,1)S(1)}, bf16[4,128,1792]{2,1,0:T(8,128)(2,1)}, u32[]{:S(2)}, u32[]{:S(2)}) collective-permute-start(bf16[4,128,1792]{2,1,0:T(8,128)(2,1)S(1)} %all-to-all-done), channel_id=1, source_target_pairs={{0,1},{1,0},{2,3},{3,2},{4,5},{5,4},{6,7},{7,6},{8,9},{9,8},{10,11... | collective-permute-start | bytes 5505032 | tf_op jit(solution)/shard_map/ppermute | solution.py:92
  175.1 5.1 collective-permute-start.1
  207.8 1.0 copy-start
  207.8 1.2 copy-start.7
  210.6 3.7 copy-start.2
  210.6 3.8 copy-start.4
  210.6 26.0 %all-to-all-start.3 = ((bf16[4,128,1792]{2,1,0:T(8,128)(2,1)}), bf16[4,128,1792]{2,1,0:T(8,128)(2,1)S(1)}, u32[]{:S(2)}, u32[]{:S(2)}) async-start(bf16[4,128,1792]{2,1,0:T(8,128)(2,1)} %tile.5), calls=%async_computation.3 | async-start | bytes 3670016 | tf_op jit(solution)/shard_map/all_to_all | solution.py:156
  241.0 222.3 %all-to-all-start.4 = ((bf16[32,56,2688]{2,1,0:T(8,128)(2,1)}), bf16[32,56,2688]{2,1,0:T(8,128)(2,1)}, u32[]{:S(2)}, u32[]{:S(2)}) async-start(bf16[32,56,2688]{2,1,0:T(8,128)(2,1)} %stack.16), calls=%async_computation.4 | async-start | bytes 19267584 | tf_op jit(solution)/shard_map/all_to_all | solution.py:78
  245.9 268.4 %reduce-scatter.2.cloned.1.call-start = ((), (), s32[]{:S(2)}) async-start(), calls=%async_computation.7 | async-start | bytes 1146880 | tf_op jit(solution)/shard_map/reduce_scatter | solution.py:166
  246.0 6.0 %collective-permute-start.2 = (bf16[512,1792]{1,0:T(8,128)(2,1)S(1)}, bf16[512,1792]{1,0:T(8,128)(2,1)}, u32[]{:S(2)}, u32[]{:S(2)}) collective-permute-start(bf16[512,1792]{1,0:T(8,128)(2,1)S(1)} %bitcast.72), channel_id=1, source_target_pairs={{0,1},{1,0},{2,3},{3,2},{4,5},{5,4},{6,7},{7,6},{8,9},{9,8},{10,11... | collective-permute-start | bytes 5505032 | tf_op jit(solution)/shard_map/ppermute | solution.py:92
  474.4 7.8 %collective-permute-start.3 = (bf16[512,1792]{1,0:T(8,128)(2,1)S(1)}, bf16[512,1792]{1,0:T(8,128)(2,1)S(1)}, u32[]{:S(2)}, u32[]{:S(2)}) collective-permute-start(bf16[512,1792]{1,0:T(8,128)(2,1)S(1)} %convolution_convert_fusion.2), channel_id=1, source_target_pairs={{0,1},{1,0},{2,3},{3,2},{4,5},{5,4},{6,7},{7,6},{8,9},{9,8},{10,11... | collective-permute-start | bytes 5505032 | tf_op jit(solution)/shard_map/ppermute | solution.py:92
  487.9 5.5 %copy-start.1 = (bf16[1,1024,224]{1,2,0:T(8,128)(2,1)S(1)}, bf16[1,1024,224]{1,2,0:T(8,128)(2,1)}, u32[]{:S(2)}) copy-start(bf16[1,1024,224]{1,2,0:T(8,128)(2,1)} %get-tuple-element.10) | copy-start | bytes 1376260
  487.9 23.4 %all-to-all-start.5 = ((bf16[4,128,896]{2,1,0:T(8,128)(2,1)}), bf16[4,128,896]{2,1,0:T(8,128)(2,1)}, u32[]{:S(2)}, u32[]{:S(2)}) async-start(bf16[4,128,896]{2,1,0:T(8,128)(2,1)} %bitcast.24), calls=%async_computation.6 | async-start | bytes 1835008 | tf_op jit(solution)/shard_map/all_to_all | solution.py:167
Sparse Core Ops, SparseCore 0:
  488.0 26.2 reduce-scatter.1
